TPU v7x, 512 devices: a whole 4x8x8 slice. The times are simulated.
512 devices in a mesh: dp: 16 (over z, core), expert: 32 (over x, y).
Axes of the slice: x: 4, y: 8, z: 8, core: 2. Of those that a mesh axis runs over, the one named last changes fastest.
Arguments:
- residual_in: bfloat16 [16384, 2048], P(('dp', 'expert')), may hold values from -6 to 6
- attention_out: bfloat16 [16384, 2048], P(('dp', 'expert')), may hold values from -6 to 6
- out_weight: bfloat16 [2048, 2048], P(None, 'dp'), may hold values from -0.125 to 0.125
- post_gain: float32 [2048], replicated, may hold values from 0.1 to 1.9
- router_weight: bfloat16 [2048, 32], replicated, may hold values from -0.125 to 0.125
- expert_ids: int32 [16384, 6], P(('dp', 'expert')), may hold values from 0 to 31, all different within a row; in each aligned block of 32 rows (0 to 31, 32 to 63, ...) at most 12 rows name the same one
- expert_slot: int32 [32], replicated, may hold values from 0 to 31, each once
- expert_gate_up: bfloat16 [32, 2048, 1408], P('expert', 'dp'), may hold values from -0.125 to 0.125
- expert_down: bfloat16 [32, 704, 2048], P('expert', None, 'dp'), may hold values from -0.21875 to 0.21875
- shared_gate_up: bfloat16 [2048, 2, 2816], P(None, None, 'dp'), may hold values from -0.125 to 0.125
- shared_down: bfloat16 [2816, 2048], P(None, 'dp'), may hold values from -0.109375 to 0.109375
- final_gain: float32 [2048], replicated, may hold values from 0.1 to 1.9
Outputs:
- mixed: bfloat16 [16384, 2048], P(('dp', 'expert'))
Inputs may be any that keep to these rules, and one draw needn't show every extreme that they name: `expert_ids`: each row names 6 different experts. In each aligned block of 32 rows (the rows of one device) no expert is named by more than 12 rows, a bound that some block reaches. A permutation: expert e is held in slot expert_slot[e].
All inputs are finite; a program needn't handle non-finite values.
Results may differ from a plain program's by a relative error of at most 0.0069.
Values may be sent and summed in bfloat16 or wider, within the bound.
No kernel may reach another device: no remote copies, remote signals or barrier semaphores. Data moves between devices by JAX's collectives and lax.ppermute only.
A program may use at most 64 MiB of HBM per device.

v0:
```python
import jax
import jax.numpy as jnp
from jax import lax
from jax.sharding import PartitionSpec as P

EPS = 1e-06


def core_groups(axis):
    n = lax.axis_size(axis)
    return [list(range(0, n, 2)), list(range(1, n, 2))]


def with_sibling(blocks, axis):
    other = lax.ppermute(blocks, axis, [(i, i ^ 1) for i in range(lax.axis_size(axis))])
    pair = jnp.stack([blocks, other], axis=1)
    pair = jnp.where(lax.axis_index(axis) % 2 == 0, pair, jnp.flip(pair, axis=1))
    return pair.reshape(-1, *blocks.shape[1:])


def pair_gather(array, axis):
    blocks = lax.all_gather(array, axis, axis=0, axis_index_groups=core_groups(axis))
    return with_sibling(blocks, axis)


def pair_collect(array, axis):
    copies = jnp.broadcast_to(array, (lax.axis_size(axis) // 2, *array.shape))
    blocks = lax.all_to_all(copies, axis, 0, 0, tiled=True, axis_index_groups=core_groups(axis))
    return with_sibling(blocks, axis)


def in_order(blocks, dim):
    shape = list(blocks.shape[1:])
    shape[dim] *= blocks.shape[0]
    return jnp.moveaxis(blocks, 0, dim).reshape(shape)


def sent_to_all(array, axis):
    copies = jnp.broadcast_to(array, (lax.axis_size(axis), *array.shape))
    return lax.all_to_all(copies, axis, split_axis=0, concat_axis=0, tiled=True)


def collect(array, axis, dim):
    return in_order(sent_to_all(array, axis), dim)


def turned_gather(arrays, axis, dims):
    turned = [jnp.moveaxis(a, dim, 0) for a, dim in zip(arrays, dims)]
    widths = [t[0].size for t in turned]
    both = jnp.concatenate([t.reshape(-1, w) for t, w in zip(turned, widths)], axis=1)
    out = lax.all_gather(both, axis, axis=0, tiled=True)
    blocks = jnp.split(out, [sum(widths[:k]) for k in range(1, len(widths))], axis=1)
    return tuple(
        (
            jnp.moveaxis(b.reshape(-1, *t.shape[1:]), 0, dim)
            for b, t, dim in zip(blocks, turned, dims)
        )
    )


def rms_scale(values, gain):
    values = values.astype(jnp.float32)
    inverse = lax.rsqrt(jnp.mean(values * values, axis=-1, keepdims=True) + EPS)
    return values * inverse * gain


def per_device(
    residual_in,
    attention_out,
    out_weight,
    post_gain,
    router_weight,
    expert_ids,
    expert_slot,
    expert_gate_up,
    expert_down,
    shared_gate_up,
    shared_down,
    final_gain,
):
    rows = residual_in.shape[0]
    width = residual_in.shape[1]
    experts = router_weight.shape[1]
    choose = expert_ids.shape[1]
    capacity = max(2, min(rows, 2 * rows * choose // experts))
    proj_cols = jnp.dot(
        in_order(pair_collect(attention_out, "dp"), 0),
        out_weight,
        preferred_element_type=jnp.float32,
    ).astype(jnp.bfloat16)
    proj = lax.all_to_all(proj_cols, "dp", split_axis=0, concat_axis=1, tiled=True)
    resid = (residual_in.astype(jnp.float32) + proj.astype(jnp.float32)).astype(jnp.bfloat16)
    normed = rms_scale(resid, post_gain).astype(jnp.bfloat16)
    logits = jnp.dot(normed, router_weight, preferred_element_type=jnp.float32)
    expert_range = jnp.arange(experts, dtype=jnp.int32)
    ids = expert_ids + (proj_cols[0, 0] * 0).astype(expert_ids.dtype)
    picked = ids[:, :, None] == expert_range[None, None, :]
    chosen = jnp.sum(jnp.where(picked, logits[:, None, :], 0.0), axis=2)
    raised = jnp.exp(chosen)
    gates = raised / jnp.sum(raised, axis=1, keepdims=True)
    slots = jnp.sum(jnp.where(picked, expert_slot[None, None, :], 0), axis=2).reshape(-1)
    marked = (slots[:, None] == expert_range[None, :]).astype(jnp.int32)
    before = jnp.cumsum(marked, axis=0) - marked
    position = jnp.sum(before * marked, axis=1)
    target = slots * capacity + position
    placed = target[:, None] == jnp.arange(experts * capacity, dtype=jnp.int32)[None, :]
    select = jnp.any(placed.reshape(rows, choose, experts * capacity), axis=1).astype(jnp.bfloat16)
    outgoing = jnp.einsum("rs,rd->sd", select, normed, preferred_element_type=jnp.float32)
    outgoing = outgoing.astype(jnp.bfloat16).reshape(experts, capacity, width)
    hidden_units = expert_down.shape[1]
    weights_part = jnp.concatenate([expert_gate_up[0], expert_down[0].T], axis=1)
    weights_full = lax.all_gather(weights_part, "dp", axis=0, tiled=True)
    gate_up_full = weights_full[:, : 2 * hidden_units]
    down_turned_full = weights_full[:, 2 * hidden_units :]
    received = lax.all_to_all(outgoing, "expert", split_axis=0, concat_axis=0, tiled=True)
    sources, count, _ = received.shape
    flat = received.reshape(sources * count, width)
    both = jnp.dot(flat, gate_up_full, preferred_element_type=jnp.float32)
    active = (jax.nn.silu(both[:, :hidden_units]) * both[:, hidden_units:]).astype(jnp.bfloat16)
    result = lax.dot_general(
        active, down_turned_full, (((1,), (1,)), ((), ())), preferred_element_type=jnp.float32
    ).astype(jnp.bfloat16)
    result = result.reshape(sources, count, width)
    returned = lax.all_to_all(result, "expert", split_axis=0, concat_axis=0, tiled=True)
    shared_units = shared_gate_up.shape[2]
    shared_pair = shared_gate_up.reshape(width, 2 * shared_units)
    normed_shared = normed + (weights_full[0, 0] * 0 + outgoing[0, 0, 0] * 0).astype(normed.dtype)
    both = jnp.dot(
        in_order(pair_gather(normed_shared, "dp"), 0),
        shared_pair,
        preferred_element_type=jnp.float32,
    )
    shared_hidden = (jax.nn.silu(both[:, :shared_units]) * both[:, shared_units:]).astype(
        jnp.bfloat16
    )
    out_cols = jnp.dot(
        in_order(pair_gather(shared_hidden, "dp"), 1),
        shared_down,
        preferred_element_type=jnp.float32,
    )
    shared_out = lax.all_to_all(
        out_cols.astype(jnp.bfloat16), "dp", split_axis=0, concat_axis=1, tiled=True
    ).astype(jnp.float32)
    weighted = jnp.sum(placed.reshape(rows, choose, experts * capacity) * gates[:, :, None], axis=1)
    routed = jnp.dot(
        weighted,
        returned.reshape(experts * capacity, width).astype(jnp.float32),
        precision=lax.Precision.HIGHEST,
        preferred_element_type=jnp.float32,
    )
    total = resid.astype(jnp.float32) + routed + shared_out
    return rms_scale(total, final_gain).astype(jnp.bfloat16)


def solution(mesh):
    in_specs = (
        P(("dp", "expert"), None),
        P(("dp", "expert"), None),
        P(None, "dp"),
        P(),
        P(),
        P(("dp", "expert"), None),
        P(),
        P("expert", "dp", None),
        P("expert", None, "dp"),
        P(None, None, "dp"),
        P(None, "dp"),
        P(),
    )
    out_specs = P(("dp", "expert"), None)
    return jax.shard_map(
        per_device, mesh=mesh, in_specs=in_specs, out_specs=out_specs, check_vma=False
    )
```

profile of v0, /device:TPU:1, one launch (start us, length us, event | category | flops | bytes accessed | tf_op | source)
XLA Modules:
  0.0 248.7 jit_solution(5507769714941726172)
XLA Ops:
  7.7 1.8 pad_maximum_fusion.3
  9.7 44.2 %all_to_all.41 = bf16[8,32,2048]{2,1,0:T(8,128)(2,1)S(1)} all-to-all(bf16[8,32,2048]{2,1,0:T(8,128)(2,1)S(1)} %broadcast_in_dim.26), channel_id=1, replica_groups={{0,64,128,192,256,320,384,448},{32,96,160,224,288,352,416,480},{1,65,12..., dimensions={0} | all-to-all | bytes 2097152 | tf_op jit(solution)/shard_map/all_to_all | solution.py:28
  53.9 5.5 %collective-permute-start = (bf16[8,32,2048]{2,1,0:T(8,128)(2,1)S(1)}, bf16[8,32,2048]{2,1,0:T(8,128)(2,1)S(1)}, u32[]{:S(2)}, u32[]{:S(2)}) collective-permute-start(bf16[8,32,2048]{2,1,0:T(8,128)(2,1)S(1)} %all_to_all.41), channel_id=1, source_target_pairs={{0,32},{32,0},{64,96},{96,64},{128,160},{160,128},{192,224},{224,1... | collective-permute-start | bytes 3145736 | tf_op jit(solution)/shard_map/ppermute | solution.py:15
  59.5 2.3 collective-permute-done
  66.1 3.7 %all-to-all-start.1 = ((bf16[16,32,128]{2,1,0:T(8,128)(2,1)}), bf16[16,32,128]{2,1,0:T(8,128)(2,1)S(1)}, u32[]{:S(2)}, u32[]{:S(2)}) async-start(bf16[16,32,128]{2,1,0:T(8,128)(2,1)} %bitcast.4), calls=%async_computation.1 | async-start | bytes 262144 | tf_op jit(solution)/shard_map/all_to_all | solution.py:91
  71.6 8.8 %all-to-all-done.1 = bf16[16,32,128]{2,1,0:T(8,128)(2,1)S(1)} async-done(((bf16[16,32,128]{2,1,0:T(8,128)(2,1)}), bf16[16,32,128]{2,1,0:T(8,128)(2,1)S(1)}, u32[]{:S(2)}, u32[]{:S(2)}) %all-to-all-start.1) | async-done | bytes 131104 | tf_op jit(solution)/shard_map/all_to_all | solution.py:91
  81.3 1.6 reshape.112
  84.7 8.7 %all-gather.6.cloned.1.call-done = bf16[2048,2112]{1,0:T(8,128)(2,1)} async-done(((bf16[128,2112]{1,0:T(8,128)(2,1)}), bf16[2048,2112]{1,0:T(8,128)(2,1)}) %all-gather.6.cloned.1.call-update) | async-done | bytes 8650768 | tf_op jit(solution)/shard_map/all_gather | solution.py:112
  96.1 9.7 %all-to-all-start.2 = ((bf16[32,12,2048]{2,1,0:T(8,128)(2,1)}), bf16[32,12,2048]{2,1,0:T(8,128)(2,1)S(1)}, u32[]{:S(2)}, u32[]{:S(2)}) async-start(bf16[32,12,2048]{2,1,0:T(8,128)(2,1)} %reshape.112), calls=%async_computation.2 | async-start | bytes 4194304 | tf_op jit(solution)/shard_map/all_to_all | solution.py:115
  105.8 26.9 %all-gather.8.cloned.1.call-done = bf16[256,2048]{1,0:T(8,128)(2,1)} async-done(((bf16[32,2048]{1,0:T(8,128)(2,1)}), bf16[256,2048]{1,0:T(8,128)(2,1)}) %all-gather.8.cloned.1.call-update) | async-done | bytes 1048592 | tf_op jit(solution)/shard_map/all_gather | solution.py:22
  132.8 6.4 %collective-permute-start.1 = (bf16[8,32,2048]{2,1,0:T(8,128)(2,1)}, bf16[8,32,2048]{2,1,0:T(8,128)(2,1)S(1)}, u32[]{:S(2)}, u32[]{:S(2)}) collective-permute-start(bf16[8,32,2048]{2,1,0:T(8,128)(2,1)} %bitcast.86), channel_id=1, source_target_pairs={{0,32},{32,0},{64,96},{96,64},{128,160},{160,128},{192,224},{224,1... | collective-permute-start | bytes 3145736 | tf_op jit(solution)/shard_map/ppermute | solution.py:15
  139.2 2.5 collective-permute-done.1
  145.4 9.3 %all-to-all-done.2 = bf16[32,12,2048]{2,1,0:T(8,128)(2,1)S(1)} async-done(((bf16[32,12,2048]{2,1,0:T(8,128)(2,1)}), bf16[32,12,2048]{2,1,0:T(8,128)(2,1)S(1)}, u32[]{:S(2)}, u32[]{:S(2)}) %all-to-all-start.2) | async-done | bytes 1572896 | tf_op jit(solution)/shard_map/all_to_all | solution.py:115
  156.0 5.8 %fusion = f32[384,1408]{1,0:T(8,128)S(1)} fusion(bf16[384,2048]{1,0:T(8,128)(2,1)} %reshape.113, bf16[2048,2112]{1,0:T(8,128)(2,1)} %all-gather.6.cloned.1.call-done), kind=kOutput, calls=%fused_computation | convolution fusion | flops 2214592512 | bytes 9502720 | tf_op jit(solution)/shard_map/dot_general | solution.py:118
  161.8 3.3 %fusion.4 = bf16[384,2048]{1,0:T(8,128)(2,1)S(1)} fusion(bf16[2048,2112]{1,0:T(8,128)(2,1)} %all-gather.6.cloned.1.call-done, f32[384,1408]{1,0:T(8,128)S(1)} %fusion), kind=kOutput, calls=%fused_computation.8 | convolution fusion | flops 1109704704 | bytes 7077888 | tf_op jit(solution)/shard_map/dot_general | solution.py:120
  166.7 7.5 %all-to-all-start.3 = ((bf16[32,12,2048]{2,1,0:T(8,128)(2,1)}), bf16[32,12,2048]{2,1,0:T(8,128)(2,1)S(1)}, u32[]{:S(2)}, u32[]{:S(2)}) async-start(bf16[32,12,2048]{2,1,0:T(8,128)(2,1)} %reshape.114), calls=%async_computation.3 | async-start | bytes 4194304 | tf_op jit(solution)/shard_map/all_to_all | solution.py:124
  174.2 7.8 %all-gather.10.cloned.1.call-done = bf16[4096,176]{0,1:T(8,128)(2,1)} async-done(((bf16[512,176]{0,1:T(8,128)(2,1)}), bf16[4096,176]{0,1:T(8,128)(2,1)}) %all-gather.10.cloned.1.call-update) | async-done | bytes 1441808 | tf_op jit(solution)/shard_map/all_gather | solution.py:22
  182.0 1.6 copy.60
  183.6 7.3 %collective-permute-start.2 = (bf16[8,512,176]{1,2,0:T(8,128)(2,1)S(1)}, bf16[8,512,176]{1,2,0:T(8,128)(2,1)S(1)}, u32[]{:S(2)}, u32[]{:S(2)}) collective-permute-start(bf16[8,512,176]{1,2,0:T(8,128)(2,1)S(1)} %bitcast.83), channel_id=1, source_target_pairs={{0,32},{32,0},{64,96},{96,64},{128,160},{160,128},{192,224},{224,1... | collective-permute-start | bytes 4325384 | tf_op jit(solution)/shard_map/ppermute | solution.py:15
  195.0 1.6 convolution_convert_fusion.2
  196.6 26.5 %all-to-all-done.3 = bf16[32,12,2048]{2,1,0:T(8,128)(2,1)S(1)} async-done(((bf16[32,12,2048]{2,1,0:T(8,128)(2,1)}), bf16[32,12,2048]{2,1,0:T(8,128)(2,1)S(1)}, u32[]{:S(2)}, u32[]{:S(2)}) %all-to-all-start.3) | async-done | bytes 1572896 | tf_op jit(solution)/shard_map/all_to_all | solution.py:124
  223.1 6.7 %all-to-all-start.4 = ((bf16[16,32,128]{2,1,0:T(8,128)(2,1)}), bf16[16,32,128]{2,1,0:T(8,128)(2,1)}, u32[]{:S(2)}, u32[]{:S(2)}) async-start(bf16[16,32,128]{2,1,0:T(8,128)(2,1)} %bitcast.90), calls=%async_computation.4 | async-start | bytes 262144 | tf_op jit(solution)/shard_map/all_to_all | solution.py:141
  231.8 7.2 %all-to-all-done.4 = bf16[16,32,128]{2,1,0:T(8,128)(2,1)} async-done(((bf16[16,32,128]{2,1,0:T(8,128)(2,1)}), bf16[16,32,128]{2,1,0:T(8,128)(2,1)}, u32[]{:S(2)}, u32[]{:S(2)}) %all-to-all-start.4) | async-done | bytes 131104 | tf_op jit(solution)/shard_map/all_to_all | solution.py:141
  239.0 2.4 multiply_reduce_fusion
  (83 shorter events, 24.2 us)
Async XLA Ops:
  6.5 137.1 %copy-start = (bf16[2048,2,176]{0,2,1:T(8,128)(2,1)S(1)}, bf16[2048,2,176]{0,2,1:T(8,128)(2,1)}, u32[]{:S(2)}) copy-start(bf16[2048,2,176]{0,2,1:T(8,128)(2,1)} %param.21) | copy-start | bytes 4325380
  6.5 3.0 %copy-start.6 = (bf16[32,2048]{1,0:T(8,128)(2,1)S(1)}, bf16[32,2048]{1,0:T(8,128)(2,1)}, u32[]{:S(2)}) copy-start(bf16[32,2048]{1,0:T(8,128)(2,1)} %param.13) | copy-start | bytes 393220
  6.5 86.9 %all-gather.6.cloned.1.call-start = ((), (), s32[]{:S(2)}) async-start(), calls=%async_computation.5 | async-start | bytes 9469952 | tf_op jit(solution)/shard_map/all_gather | solution.py:112
  53.9 7.8 %collective-permute-start = (bf16[8,32,2048]{2,1,0:T(8,128)(2,1)S(1)}, bf16[8,32,2048]{2,1,0:T(8,128)(2,1)S(1)}, u32[]{:S(2)}, u32[]{:S(2)}) collective-permute-start(bf16[8,32,2048]{2,1,0:T(8,128)(2,1)S(1)} %all_to_all.41), channel_id=1, source_target_pairs={{0,32},{32,0},{64,96},{96,64},{128,160},{160,128},{192,224},{224,1... | collective-permute-start | bytes 3145736 | tf_op jit(solution)/shard_map/ppermute | solution.py:15
  62.5 7.3 %copy-start.10 = (s32[32,6]{0,1:T(8,128)S(1)}, s32[32,6]{0,1:T(8,128)}, u32[]{:S(2)}) copy-start(s32[32,6]{0,1:T(8,128)} %param.17) | copy-start | bytes 2308
  62.6 7.3 %copy-start.13 = (s32[32]{0:T(128)S(1)}, s32[32]{0:T(128)}, u32[]{:S(2)}) copy-start(s32[32]{0:T(128)} %param.18) | copy-start | bytes 388
  62.6 17.9 %copy-start.7 = (bf16[32,2048]{1,0:T(8,128)(2,1)S(1)}, bf16[32,2048]{1,0:T(8,128)(2,1)}, u32[]{:S(2)}) copy-start(bf16[32,2048]{1,0:T(8,128)(2,1)} %param.12) | copy-start | bytes 393220
  62.6 18.1 %copy-start.8 = (f32[2048]{0:T(1024)S(1)}, f32[2048]{0:T(1024)}, u32[]{:S(2)}) copy-start(f32[2048]{0:T(1024)} %param.15) | copy-start | bytes 24580
  66.1 14.4 %all-to-all-start.1 = ((bf16[16,32,128]{2,1,0:T(8,128)(2,1)}), bf16[16,32,128]{2,1,0:T(8,128)(2,1)S(1)}, u32[]{:S(2)}, u32[]{:S(2)}) async-start(bf16[16,32,128]{2,1,0:T(8,128)(2,1)} %bitcast.4), calls=%async_computation.1 | async-start | bytes 262144 | tf_op jit(solution)/shard_map/all_to_all | solution.py:91
  69.8 63.0 %all-gather.8.cloned.1.call-start = ((), (), s32[]{:S(2)}) async-start(), calls=%async_computation.6 | async-start | bytes 1179648 | tf_op jit(solution)/shard_map/all_gather | solution.py:22
  80.6 14.7 %copy-start.2 = (bf16[32,2048]{1,0:T(8,128)(2,1)}, bf16[32,2048]{1,0:T(8,128)(2,1)S(1)}, u32[]{:S(2)}) copy-start(bf16[32,2048]{1,0:T(8,128)(2,1)S(1)} %get-tuple-element.6) | copy-start | bytes 393220
  80.6 14.6 %copy-start.11 = (f32[32]{0:T(128)}, f32[32]{0:T(128)S(1)}, u32[]{:S(2)}) copy-start(f32[32]{0:T(128)S(1)} %add_rsqrt_fusion.1) | copy-start | bytes 388
  96.1 58.6 %all-to-all-start.2 = ((bf16[32,12,2048]{2,1,0:T(8,128)(2,1)}), bf16[32,12,2048]{2,1,0:T(8,128)(2,1)S(1)}, u32[]{:S(2)}, u32[]{:S(2)}) async-start(bf16[32,12,2048]{2,1,0:T(8,128)(2,1)} %reshape.112), calls=%async_computation.2 | async-start | bytes 4194304 | tf_op jit(solution)/shard_map/all_to_all | solution.py:115
  105.8 76.3 %all-gather.10.cloned.1.call-start = ((), (), s32[]{:S(2)}) async-start(), calls=%async_computation.7 | async-start | bytes 1622016 | tf_op jit(solution)/shard_map/all_gather | solution.py:22
  132.8 8.9 %collective-permute-start.1 = (bf16[8,32,2048]{2,1,0:T(8,128)(2,1)}, bf16[8,32,2048]{2,1,0:T(8,128)(2,1)S(1)}, u32[]{:S(2)}, u32[]{:S(2)}) collective-permute-start(bf16[8,32,2048]{2,1,0:T(8,128)(2,1)} %bitcast.86), channel_id=1, source_target_pairs={{0,32},{32,0},{64,96},{96,64},{128,160},{160,128},{192,224},{224,1... | collective-permute-start | bytes 3145736 | tf_op jit(solution)/shard_map/ppermute | solution.py:15
  166.7 56.4 %all-to-all-start.3 = ((bf16[32,12,2048]{2,1,0:T(8,128)(2,1)}), bf16[32,12,2048]{2,1,0:T(8,128)(2,1)S(1)}, u32[]{:S(2)}, u32[]{:S(2)}) async-start(bf16[32,12,2048]{2,1,0:T(8,128)(2,1)} %reshape.114), calls=%async_computation.3 | async-start | bytes 4194304 | tf_op jit(solution)/shard_map/all_to_all | solution.py:124
  182.0 8.9 %copy-start.3 = (bf16[32,2048]{1,0:T(8,128)(2,1)S(1)}, bf16[32,2048]{1,0:T(8,128)(2,1)}, u32[]{:S(2)}) copy-start(bf16[32,2048]{1,0:T(8,128)(2,1)} %copy-done.2) | copy-start | bytes 393220
  182.0 8.9 %copy-start.12 = (f32[32]{0:T(128)S(1)}, f32[32]{0:T(128)}, u32[]{:S(2)}) copy-start(f32[32]{0:T(128)} %copy-done.11) | copy-start | bytes 388
  182.0 8.9 %copy-start.14 = (bf16[2048,32]{0,1:T(8,128)(2,1)S(1)}, bf16[2048,32]{0,1:T(8,128)(2,1)}, u32[]{:S(2)}) copy-start(bf16[2048,32]{0,1:T(8,128)(2,1)} %param.16) | copy-start | bytes 393220
  182.0 9.4 %copy-start.1 = (bf16[4096,176]{0,1:T(8,128)(2,1)S(1)}, bf16[4096,176]{0,1:T(8,128)(2,1)}, u32[]{:S(2)}) copy-start(bf16[4096,176]{0,1:T(8,128)(2,1)} %all-gather.10.cloned.1.call-done) | copy-start | bytes 4325380
  183.6 9.9 %collective-permute-start.2 = (bf16[8,512,176]{1,2,0:T(8,128)(2,1)S(1)}, bf16[8,512,176]{1,2,0:T(8,128)(2,1)S(1)}, u32[]{:S(2)}, u32[]{:S(2)}) collective-permute-start(bf16[8,512,176]{1,2,0:T(8,128)(2,1)S(1)} %bitcast.83), channel_id=1, source_target_pairs={{0,32},{32,0},{64,96},{96,64},{128,160},{160,128},{192,224},{224,1... | collective-permute-start | bytes 4325384 | tf_op jit(solution)/shard_map/ppermute | solution.py:15
  193.9 1.1 copy-start.4
  223.1 16.0 %all-to-all-start.4 = ((bf16[16,32,128]{2,1,0:T(8,128)(2,1)}), bf16[16,32,128]{2,1,0:T(8,128)(2,1)}, u32[]{:S(2)}, u32[]{:S(2)}) async-start(bf16[16,32,128]{2,1,0:T(8,128)(2,1)} %bitcast.90), calls=%async_computation.4 | async-start | bytes 262144 | tf_op jit(solution)/shard_map/all_to_all | solution.py:141
  230.5 10.9 %copy-start.9 = (f32[2048]{0:T(1024)S(1)}, f32[2048]{0:T(1024)}, u32[]{:S(2)}) copy-start(f32[2048]{0:T(1024)} %param.23) | copy-start | bytes 24580
  (1 other events, 1.0 us)
Sparse Core Ops, SparseCore 0:
  9.7 83.6 all-gather.5
  96.2 36.5 all-gather.7
  145.5 36.4 all-gather.9
where the time goes:
time: 250 us; the launch traced here: 249 us
  waiting for transfers between devices  101 us (40%)
  starting transfers between devices  46.9 us (19%)
  blocking collectives  44.2 us (18%)
  matrix products  16.3 us (7%)
  between operations  15.4 us (6%)
  local copies, waits for them, and re-layouts  14.8 us (6%)
  other arithmetic  9.99 us (4%)
    all_to_all x1, blocking collectives, pair_collect(): lax.all_to_all(copies, axis, 0, 0, tiled=True, axis_index_groups=core_gro...  44.2 us
    all_gather x2, waiting for transfers between devices, pair_gather(): lax.all_gather(array, axis, axis=0, axis_index_groups=core_groups(axis))  34.7 us
    all_to_all x1, waiting for transfers between devices, per_device(): lax.all_to_all(result, 'expert', split_axis=0, concat_axis=0, tiled=True)  26.5 us
    ppermute x3, starting transfers between devices, with_sibling(): lax.ppermute(blocks, axis, [(i, i ^ 1) for i in range(lax.axis_size(axis))])  19.2 us
    all_to_all x1, starting transfers between devices, per_device(): lax.all_to_all(outgoing, 'expert', split_axis=0, concat_axis=0, tiled=True)  9.68 us
    all_to_all x1, waiting for transfers between devices, per_device(): lax.all_to_all(outgoing, 'expert', split_axis=0, concat_axis=0, tiled=True)  9.27 us
    all_to_all x1, waiting for transfers between devices, per_device(): lax.all_to_all(proj_cols, 'dp', split_axis=0, concat_axis=1, tiled=True)  8.85 us
    all_gather x1, waiting for transfers between devices, per_device(): weights_full = lax.all_gather(weights_part, 'dp', axis=0, tiled=True)  8.74 us
  transfers between devices with their start and end apart: 10, of which 10 were waited for; matrix products, arithmetic and copies ran while one was open for 13% of the time, Pallas kernels for 0%

commit v1 on v0

--- a/solution.py
+++ b/solution.py
@@ -2,6 +2,7 @@
 import jax.numpy as jnp
 from jax import lax
 from jax.sharding import PartitionSpec as P
+from jax.lax import all_to_all, psum
 
 EPS = 1e-06
 
@@ -109,7 +110,9 @@
     outgoing = outgoing.astype(jnp.bfloat16).reshape(experts, capacity, width)
     hidden_units = expert_down.shape[1]
     weights_part = jnp.concatenate([expert_gate_up[0], expert_down[0].T], axis=1)
-    weights_full = lax.all_gather(weights_part, "dp", axis=0, tiled=True)
+    weights_full = jnp.concatenate(
+        all_to_all(jnp.stack([weights_part] * psum(1, "dp")), "dp", 0, 0), axis=0
+    )
     gate_up_full = weights_full[:, : 2 * hidden_units]
     down_turned_full = weights_full[:, 2 * hidden_units :]
     received = lax.all_to_all(outgoing, "expert", split_axis=0, concat_axis=0, tiled=True)

time: 250 us -> 435 us (1.74)
  waiting for transfers between devices: 101 us -> 271 us
  local copies, waits for them, and re-layouts: 14.8 us -> 33.5 us
  blocking collectives: 44.2 us -> 37.9 us
    all_to_all x0 -> x1, waiting for transfers between devices: none -> 181 us  [per_device(): all_to_all(jnp.stack([weights_part] * psum(1, 'dp')), 'dp', 0, 0)]
    all_to_all x0 -> x1, local copies, waits for them, and re-layouts: none -> 11.7 us  [per_device(): all_to_all(jnp.stack([weights_part] * psum(1, 'dp')), 'dp', 0, 0)]
    all_gather x1 -> x0, waiting for transfers between devices: 8.74 us -> none  [per_device(): weights_full = lax.all_gather(weights_part, 'dp', axis=0, tiled=True)]
    all_to_all x1, blocking collectives: 44.2 us -> 37.9 us  [pair_collect(): lax.all_to_all(copies, axis, 0, 0, tiled=True, axis_index_groups=core_gro...]
    another operation x1 -> x2, local copies, waits for them, and re-layouts: 0.01 us -> 5 us  [the longest x1 4.99 us: per_device(): jnp.stack([weights_part] * psum(1, 'dp'))]
    all_to_all x0 -> x1, starting transfers between devices: none -> 4.79 us  [per_device(): all_to_all(jnp.stack([weights_part] * psum(1, 'dp')), 'dp', 0, 0)]
  transfers between devices with their start and end apart: 10 -> 10, of which waited for: 10 -> 10; matrix products, arithmetic and copies ran while one was open for 13% -> 7% of each run, Pallas kernels for 0% -> 0%
where the time goes in v1:
time: 435 us; the launch traced here: 434 us
  waiting for transfers between devices  271 us (62%)
  starting transfers between devices  51.2 us (12%)
  blocking collectives  37.9 us (9%)
  local copies, waits for them, and re-layouts  33.5 us (8%)
  matrix products  16.3 us (4%)
  between operations  15.8 us (4%)
  other arithmetic  8.19 us (2%)
    all_to_all x1, waiting for transfers between devices, per_device(): all_to_all(jnp.stack([weights_part] * psum(1, 'dp')), 'dp', 0, 0)  181 us
    all_to_all x1, blocking collectives, pair_collect(): lax.all_to_all(copies, axis, 0, 0, tiled=True, axis_index_groups=core_gro...  37.9 us
    all_gather x2, waiting for transfers between devices, pair_gather(): lax.all_gather(array, axis, axis=0, axis_index_groups=core_groups(axis))  36.8 us
    all_to_all x1, waiting for transfers between devices, per_device(): lax.all_to_all(result, 'expert', split_axis=0, concat_axis=0, tiled=True)  24.9 us
    ppermute x3, starting transfers between devices, with_sibling(): lax.ppermute(blocks, axis, [(i, i ^ 1) for i in range(lax.axis_size(axis))])  18.4 us
    all_to_all x1, local copies, waits for them, and re-layouts, per_device(): all_to_all(jnp.stack([weights_part] * psum(1, 'dp')), 'dp', 0, 0)  11.7 us
    all_to_all x1, starting transfers between devices, per_device(): lax.all_to_all(outgoing, 'expert', split_axis=0, concat_axis=0, tiled=True)  9.68 us
    all_to_all x1, waiting for transfers between devices, per_device(): lax.all_to_all(proj_cols, 'dp', split_axis=0, concat_axis=1, tiled=True)  8.86 us
  transfers between devices with their start and end apart: 10, of which 10 were waited for; matrix products, arithmetic and copies ran while one was open for 7% of the time, Pallas kernels for 0%

profile of v1, /device:TPU:1, one launch (start us, length us, event | category | flops | bytes accessed | tf_op | source)
XLA Modules:
  0.0 433.5 jit_solution(6776661390882591521)
XLA Ops:
  7.7 37.9 %all_to_all.46 = bf16[8,32,2048]{2,1,0:T(8,128)(2,1)S(1)} all-to-all(bf16[8,32,2048]{2,1,0:T(8,128)(2,1)S(1)} %broadcast_in_dim.26), channel_id=1, replica_groups={{0,64,128,192,256,320,384,448},{32,96,160,224,288,352,416,480},{1,65,12..., dimensions={0} | all-to-all | bytes 2097152 | tf_op jit(solution)/shard_map/all_to_all | solution.py:29
  45.6 4.4 %collective-permute-start = (bf16[8,32,2048]{2,1,0:T(8,128)(2,1)S(1)}, bf16[8,32,2048]{2,1,0:T(8,128)(2,1)S(1)}, u32[]{:S(2)}, u32[]{:S(2)}) collective-permute-start(bf16[8,32,2048]{2,1,0:T(8,128)(2,1)S(1)} %all_to_all.46), channel_id=1, source_target_pairs={{0,32},{32,0},{64,96},{96,64},{128,160},{160,128},{192,224},{224,1... | collective-permute-start | bytes 3145736 | tf_op jit(solution)/shard_map/ppermute | solution.py:16
  49.9 1.7 copy.45
  54.8 3.7 all-to-all-start.1
  58.8 8.9 %all-to-all-done.1 = bf16[16,32,128]{2,1,0:T(8,128)(2,1)S(1)} async-done(((bf16[16,32,128]{2,1,0:T(8,128)(2,1)}), bf16[16,32,128]{2,1,0:T(8,128)(2,1)S(1)}, u32[]{:S(2)}, u32[]{:S(2)}) %all-to-all-start.1) | async-done | bytes 131104 | tf_op jit(solution)/shard_map/all_to_all | solution.py:92
  67.7 5.0 %stack.23 = bf16[16,128,2112]{1,2,0:T(8,128)(2,1)} broadcast(bf16[128,2112]{0,1:T(8,128)(2,1)S(1)} %copy.46), dimensions={1,2} | broadcast | bytes 9191424 | tf_op jit(solution)/shard_map/stack | solution.py:114
  72.7 4.8 %all-to-all-start.3 = ((bf16[16,128,2112]{1,2,0:T(8,128)(2,1)}), bf16[16,128,2112]{1,2,0:T(8,128)(2,1)}, u32[]{:S(2)}, u32[]{:S(2)}) async-start(bf16[16,128,2112]{1,2,0:T(8,128)(2,1)} %stack.23), calls=%async_computation.3 | async-start | bytes 17301504 | tf_op jit(solution)/shard_map/all_to_all | solution.py:114
  85.6 180.6 %all-to-all-done.3 = bf16[16,128,2112]{1,2,0:T(8,128)(2,1)} async-done(((bf16[16,128,2112]{1,2,0:T(8,128)(2,1)}), bf16[16,128,2112]{1,2,0:T(8,128)(2,1)}, u32[]{:S(2)}, u32[]{:S(2)}) %all-to-all-start.3) | async-done | bytes 8650784 | tf_op jit(solution)/shard_map/all_to_all | solution.py:114
  266.2 11.7 %copy.47 = bf16[16,128,2112]{2,1,0:T(8,128)(2,1)} copy(bf16[16,128,2112]{1,2,0:T(8,128)(2,1)} %all-to-all-done.3) | data formatting | bytes 17301504 | tf_op jit(solution)/shard_map/all_to_all | solution.py:114
  280.5 9.7 %all-to-all-start.2 = ((bf16[32,12,2048]{2,1,0:T(8,128)(2,1)}), bf16[32,12,2048]{2,1,0:T(8,128)(2,1)S(1)}, u32[]{:S(2)}, u32[]{:S(2)}) async-start(bf16[32,12,2048]{2,1,0:T(8,128)(2,1)} %reshape.117), calls=%async_computation.2 | async-start | bytes 4194304 | tf_op jit(solution)/shard_map/all_to_all | solution.py:118
  290.3 27.6 %all-gather.5.cloned.1.call-done = bf16[256,2048]{1,0:T(8,128)(2,1)} async-done(((bf16[32,2048]{1,0:T(8,128)(2,1)}), bf16[256,2048]{1,0:T(8,128)(2,1)}) %all-gather.5.cloned.1.call-update) | async-done | bytes 1048592 | tf_op jit(solution)/shard_map/all_gather | solution.py:23
  317.9 6.7 %collective-permute-start.1 = (bf16[8,32,2048]{2,1,0:T(8,128)(2,1)}, bf16[8,32,2048]{2,1,0:T(8,128)(2,1)S(1)}, u32[]{:S(2)}, u32[]{:S(2)}) collective-permute-start(bf16[8,32,2048]{2,1,0:T(8,128)(2,1)} %bitcast.90), channel_id=1, source_target_pairs={{0,32},{32,0},{64,96},{96,64},{128,160},{160,128},{192,224},{224,1... | collective-permute-start | bytes 3145736 | tf_op jit(solution)/shard_map/ppermute | solution.py:16
  324.6 2.5 collective-permute-done.1
  330.9 8.1 %all-to-all-done.2 = bf16[32,12,2048]{2,1,0:T(8,128)(2,1)S(1)} async-done(((bf16[32,12,2048]{2,1,0:T(8,128)(2,1)}), bf16[32,12,2048]{2,1,0:T(8,128)(2,1)S(1)}, u32[]{:S(2)}, u32[]{:S(2)}) %all-to-all-start.2) | async-done | bytes 1572896 | tf_op jit(solution)/shard_map/all_to_all | solution.py:118
  340.3 5.8 %fusion = f32[384,1408]{1,0:T(8,128)S(1)} fusion(bf16[384,2048]{1,0:T(8,128)(2,1)} %reshape.118, bf16[2048,2112]{1,0:T(8,128)(2,1)} %bitcast.79), kind=kOutput, calls=%fused_computation | convolution fusion | flops 2214592512 | bytes 9502720 | tf_op jit(solution)/shard_map/dot_general | solution.py:121
  346.1 3.3 fusion.4
  350.9 7.0 %all-to-all-start.4 = ((bf16[32,12,2048]{2,1,0:T(8,128)(2,1)}), bf16[32,12,2048]{2,1,0:T(8,128)(2,1)S(1)}, u32[]{:S(2)}, u32[]{:S(2)}) async-start(bf16[32,12,2048]{2,1,0:T(8,128)(2,1)} %reshape.120), calls=%async_computation.4 | async-start | bytes 4194304 | tf_op jit(solution)/shard_map/all_to_all | solution.py:127
  358.0 9.1 %all-gather.7.cloned.1.call-done = bf16[4096,176]{0,1:T(8,128)(2,1)} async-done(((bf16[512,176]{0,1:T(8,128)(2,1)}), bf16[4096,176]{0,1:T(8,128)(2,1)}) %all-gather.7.cloned.1.call-update) | async-done | bytes 1441808 | tf_op jit(solution)/shard_map/all_gather | solution.py:23
  368.8 7.3 %collective-permute-start.2 = (bf16[8,512,176]{1,2,0:T(8,128)(2,1)S(1)}, bf16[8,512,176]{1,2,0:T(8,128)(2,1)S(1)}, u32[]{:S(2)}, u32[]{:S(2)}) collective-permute-start(bf16[8,512,176]{1,2,0:T(8,128)(2,1)S(1)} %bitcast.87), channel_id=1, source_target_pairs={{0,32},{32,0},{64,96},{96,64},{128,160},{160,128},{192,224},{224,1... | collective-permute-start | bytes 4325384 | tf_op jit(solution)/shard_map/ppermute | solution.py:16
  380.1 1.6 convolution_convert_fusion.2
  381.7 24.9 %all-to-all-done.4 = bf16[32,12,2048]{2,1,0:T(8,128)(2,1)S(1)} async-done(((bf16[32,12,2048]{2,1,0:T(8,128)(2,1)}), bf16[32,12,2048]{2,1,0:T(8,128)(2,1)S(1)}, u32[]{:S(2)}, u32[]{:S(2)}) %all-to-all-start.4) | async-done | bytes 1572896 | tf_op jit(solution)/shard_map/all_to_all | solution.py:127
  406.6 7.6 %all-to-all-start.5 = ((bf16[16,32,128]{2,1,0:T(8,128)(2,1)}), bf16[16,32,128]{2,1,0:T(8,128)(2,1)}, u32[]{:S(2)}, u32[]{:S(2)}) async-start(bf16[16,32,128]{2,1,0:T(8,128)(2,1)} %bitcast.24), calls=%async_computation.5 | async-start | bytes 262144 | tf_op jit(solution)/shard_map/all_to_all | solution.py:144
  416.3 7.2 %all-to-all-done.5 = bf16[16,32,128]{2,1,0:T(8,128)(2,1)} async-done(((bf16[16,32,128]{2,1,0:T(8,128)(2,1)}), bf16[16,32,128]{2,1,0:T(8,128)(2,1)}, u32[]{:S(2)}, u32[]{:S(2)}) %all-to-all-start.5) | async-done | bytes 131104 | tf_op jit(solution)/shard_map/all_to_all | solution.py:144
  423.5 2.4 multiply_reduce_fusion
  (89 shorter events, 28.2 us)
Async XLA Ops:
  6.5 322.6 %copy-start = (bf16[2048,2,176]{0,2,1:T(8,128)(2,1)S(1)}, bf16[2048,2,176]{0,2,1:T(8,128)(2,1)}, u32[]{:S(2)}) copy-start(bf16[2048,2,176]{0,2,1:T(8,128)(2,1)} %param.21) | copy-start | bytes 4325380
  45.6 6.6 %collective-permute-start = (bf16[8,32,2048]{2,1,0:T(8,128)(2,1)S(1)}, bf16[8,32,2048]{2,1,0:T(8,128)(2,1)S(1)}, u32[]{:S(2)}, u32[]{:S(2)}) collective-permute-start(bf16[8,32,2048]{2,1,0:T(8,128)(2,1)S(1)} %all_to_all.46), channel_id=1, source_target_pairs={{0,32},{32,0},{64,96},{96,64},{128,160},{160,128},{192,224},{224,1... | collective-permute-start | bytes 3145736 | tf_op jit(solution)/shard_map/ppermute | solution.py:16
  53.0 5.5 %copy-start.5 = (bf16[128,704]{1,0:T(8,128)(2,1)S(1)}, bf16[128,704]{1,0:T(8,128)(2,1)}, u32[]{:S(2)}) copy-start(bf16[128,704]{1,0:T(8,128)(2,1)} %copy.45) | copy-start | bytes 540676
  54.8 12.9 %all-to-all-start.1 = ((bf16[16,32,128]{2,1,0:T(8,128)(2,1)}), bf16[16,32,128]{2,1,0:T(8,128)(2,1)S(1)}, u32[]{:S(2)}, u32[]{:S(2)}) async-start(bf16[16,32,128]{2,1,0:T(8,128)(2,1)} %bitcast.4), calls=%async_computation.1 | async-start | bytes 262144 | tf_op jit(solution)/shard_map/all_to_all | solution.py:92
  72.7 6.8 %copy-start.12 = (s32[32,6]{0,1:T(8,128)S(1)}, s32[32,6]{0,1:T(8,128)}, u32[]{:S(2)}) copy-start(s32[32,6]{0,1:T(8,128)} %param.17) | copy-start | bytes 2308
  72.7 6.8 %copy-start.15 = (s32[32]{0:T(128)S(1)}, s32[32]{0:T(128)}, u32[]{:S(2)}) copy-start(s32[32]{0:T(128)} %param.18) | copy-start | bytes 388
  72.7 8.6 %copy-start.9 = (bf16[32,2048]{1,0:T(8,128)(2,1)S(1)}, bf16[32,2048]{1,0:T(8,128)(2,1)}, u32[]{:S(2)}) copy-start(bf16[32,2048]{1,0:T(8,128)(2,1)} %param.12) | copy-start | bytes 393220
  72.7 8.8 %copy-start.10 = (f32[2048]{0:T(1024)S(1)}, f32[2048]{0:T(1024)}, u32[]{:S(2)}) copy-start(f32[2048]{0:T(1024)} %param.15) | copy-start | bytes 24580
  72.7 193.6 %all-to-all-start.3 = ((bf16[16,128,2112]{1,2,0:T(8,128)(2,1)}), bf16[16,128,2112]{1,2,0:T(8,128)(2,1)}, u32[]{:S(2)}, u32[]{:S(2)}) async-start(bf16[16,128,2112]{1,2,0:T(8,128)(2,1)} %stack.23), calls=%async_computation.3 | async-start | bytes 17301504 | tf_op jit(solution)/shard_map/all_to_all | solution.py:114
  77.5 240.4 %all-gather.5.cloned.1.call-start = ((), (), s32[]{:S(2)}) async-start(), calls=%async_computation.6 | async-start | bytes 1179648 | tf_op jit(solution)/shard_map/all_gather | solution.py:23
  81.4 198.3 %copy-start.3 = (bf16[32,2048]{1,0:T(8,128)(2,1)}, bf16[32,2048]{1,0:T(8,128)(2,1)S(1)}, u32[]{:S(2)}) copy-start(bf16[32,2048]{1,0:T(8,128)(2,1)S(1)} %get-tuple-element.6) | copy-start | bytes 393220
  81.5 198.3 %copy-start.13 = (f32[32]{0:T(128)}, f32[32]{0:T(128)S(1)}, u32[]{:S(2)}) copy-start(f32[32]{0:T(128)S(1)} %add_rsqrt_fusion.1) | copy-start | bytes 388
  280.5 58.4 %all-to-all-start.2 = ((bf16[32,12,2048]{2,1,0:T(8,128)(2,1)}), bf16[32,12,2048]{2,1,0:T(8,128)(2,1)S(1)}, u32[]{:S(2)}, u32[]{:S(2)}) async-start(bf16[32,12,2048]{2,1,0:T(8,128)(2,1)} %reshape.117), calls=%async_computation.2 | async-start | bytes 4194304 | tf_op jit(solution)/shard_map/all_to_all | solution.py:118
  290.2 76.9 %all-gather.7.cloned.1.call-start = ((), (), s32[]{:S(2)}) async-start(), calls=%async_computation.7 | async-start | bytes 1622016 | tf_op jit(solution)/shard_map/all_gather | solution.py:23
  317.9 9.2 %collective-permute-start.1 = (bf16[8,32,2048]{2,1,0:T(8,128)(2,1)}, bf16[8,32,2048]{2,1,0:T(8,128)(2,1)S(1)}, u32[]{:S(2)}, u32[]{:S(2)}) collective-permute-start(bf16[8,32,2048]{2,1,0:T(8,128)(2,1)} %bitcast.90), channel_id=1, source_target_pairs={{0,32},{32,0},{64,96},{96,64},{128,160},{160,128},{192,224},{224,1... | collective-permute-start | bytes 3145736 | tf_op jit(solution)/shard_map/ppermute | solution.py:16
  350.9 55.7 %all-to-all-start.4 = ((bf16[32,12,2048]{2,1,0:T(8,128)(2,1)}), bf16[32,12,2048]{2,1,0:T(8,128)(2,1)S(1)}, u32[]{:S(2)}, u32[]{:S(2)}) async-start(bf16[32,12,2048]{2,1,0:T(8,128)(2,1)} %reshape.120), calls=%async_computation.4 | async-start | bytes 4194304 | tf_op jit(solution)/shard_map/all_to_all | solution.py:127
  367.1 8.9 %copy-start.4 = (bf16[32,2048]{1,0:T(8,128)(2,1)S(1)}, bf16[32,2048]{1,0:T(8,128)(2,1)}, u32[]{:S(2)}) copy-start(bf16[32,2048]{1,0:T(8,128)(2,1)} %copy-done.3) | copy-start | bytes 393220
  367.1 8.9 %copy-start.14 = (f32[32]{0:T(128)S(1)}, f32[32]{0:T(128)}, u32[]{:S(2)}) copy-start(f32[32]{0:T(128)} %copy-done.13) | copy-start | bytes 388
  367.1 8.9 %copy-start.16 = (bf16[2048,32]{0,1:T(8,128)(2,1)S(1)}, bf16[2048,32]{0,1:T(8,128)(2,1)}, u32[]{:S(2)}) copy-start(bf16[2048,32]{0,1:T(8,128)(2,1)} %param.16) | copy-start | bytes 393220
  367.1 9.4 %copy-start.2 = (bf16[4096,176]{0,1:T(8,128)(2,1)S(1)}, bf16[4096,176]{0,1:T(8,128)(2,1)}, u32[]{:S(2)}) copy-start(bf16[4096,176]{0,1:T(8,128)(2,1)} %all-gather.7.cloned.1.call-done) | copy-start | bytes 4325380
  368.8 9.9 %collective-permute-start.2 = (bf16[8,512,176]{1,2,0:T(8,128)(2,1)S(1)}, bf16[8,512,176]{1,2,0:T(8,128)(2,1)S(1)}, u32[]{:S(2)}, u32[]{:S(2)}) collective-permute-start(bf16[8,512,176]{1,2,0:T(8,128)(2,1)S(1)} %bitcast.87), channel_id=1, source_target_pairs={{0,32},{32,0},{64,96},{96,64},{128,160},{160,128},{192,224},{224,1... | collective-permute-start | bytes 4325384 | tf_op jit(solution)/shard_map/ppermute | solution.py:16
  406.6 16.9 %all-to-all-start.5 = ((bf16[16,32,128]{2,1,0:T(8,128)(2,1)}), bf16[16,32,128]{2,1,0:T(8,128)(2,1)}, u32[]{:S(2)}, u32[]{:S(2)}) async-start(bf16[16,32,128]{2,1,0:T(8,128)(2,1)} %bitcast.24), calls=%async_computation.5 | async-start | bytes 262144 | tf_op jit(solution)/shard_map/all_to_all | solution.py:144
  415.0 10.9 %copy-start.11 = (f32[2048]{0:T(1024)S(1)}, f32[2048]{0:T(1024)}, u32[]{:S(2)}) copy-start(f32[2048]{0:T(1024)} %param.23) | copy-start | bytes 24580
  415.0 11.7 %copy-start.1 = (bf16[2048,2,176]{0,2,1:T(8,128)(2,1)S(1)}, bf16[2048,2,176]{0,2,1:T(8,128)(2,1)}, u32[]{:S(2)}) copy-start(bf16[2048,2,176]{0,2,1:T(8,128)(2,1)} %param.21) | copy-start | bytes 4325380
  (3 other events, 7.7 us)
Sparse Core Ops, SparseCore 0:
  280.6 37.1 all-gather.4
  331.0 36.0 all-gather.6
